TPU v7x, 128 devices: a whole 4x4x4 slice. The times are simulated.
128 devices in a mesh: dp: 2 (over core), cent: 64 (over z, y, x).
Axes of the slice: x: 4, y: 4, z: 4, core: 2. Of those that a mesh axis runs over, the one named last changes fastest.
Arguments:
- points: bfloat16 [16384, 768], P(('dp', 'cent')), may hold values from -16 to 16
- centroids: float32 [32768, 768], P(('dp', 'cent')), may hold values from -1.5 to 1.5
Outputs:
- new_centroids: float32 [32768, 768], P(('dp', 'cent'))
- log_total: float32 [16384], P(('dp', 'cent'))
All inputs are finite; a program needn't handle non-finite values.
Results may differ from a plain program's by a relative error of at most 0.0088.
Values may be sent and summed in bfloat16 or wider, within the bound.
No kernel may reach another device: no remote copies, remote signals or barrier semaphores. Data moves between devices by JAX's collectives and lax.ppermute only.
A program may use at most 128 MiB of HBM per device.

v0:
```python
import math
import jax
import jax.numpy as jnp
from jax import lax
from jax.sharding import PartitionSpec as P

BLOCKS = 2


def score_block(members, cent_block, score_scale):
    sq_norm = jnp.sum(jnp.square(cent_block.astype(jnp.float32)), axis=1)
    products = lax.dot_general(
        members, cent_block, (((1,), (1,)), ((), ())), preferred_element_type=jnp.float32
    )
    return (2.0 * products - sq_norm[None, :]) * score_scale


def fold_stats(running, scores):
    old_max, old_sum = running
    new_max = jnp.maximum(old_max, jnp.max(scores, axis=1))
    new_sum = old_sum * jnp.exp(old_max - new_max) + jnp.sum(
        jnp.exp(scores - new_max[:, None]), axis=1
    )
    return (new_max, new_sum)


def on_device(points, centroids):
    feature_width = centroids.shape[1]
    own_rows = centroids.shape[0]
    dp_count = lax.axis_size("dp")
    score_scale = 7.0 / math.sqrt(feature_width)
    copies = centroids.astype(jnp.bfloat16)
    members = lax.all_gather(points, "cent", axis=0, tiled=True)
    member_rows = members.shape[0]
    start = (jnp.full((member_rows,), -1e30, jnp.float32), jnp.zeros((member_rows,), jnp.float32))
    part_rows = own_rows // BLOCKS
    gathered = lax.all_gather(copies, "dp", axis=0, tiled=True)
    running = start
    block_span = gathered.shape[0] // BLOCKS
    for index_j in range(BLOCKS):
        running = fold_stats(
            running,
            score_block(
                members, gathered[index_j * block_span : (index_j + 1) * block_span], score_scale
            ),
        )
    local_max, local_sum = running
    global_max = lax.pmax(local_max.astype(jnp.bfloat16), "cent").astype(local_max.dtype)
    global_sum = lax.psum(local_sum * jnp.exp(local_max - global_max), "cent")
    log_total = global_max + jnp.log(global_sum)
    arranged = gathered.reshape(dp_count, BLOCKS, part_rows, feature_width)
    sum_parts = []
    count_parts = []
    for index_j in range(BLOCKS):
        cent_block = arranged[:, index_j].reshape(dp_count * part_rows, feature_width)
        scores = score_block(members, cent_block, score_scale)
        weights = jnp.exp(scores - log_total[:, None]).astype(jnp.bfloat16)
        partial_sums = lax.dot_general(
            weights, members, (((0,), (0,)), ((), ())), preferred_element_type=jnp.float32
        )
        counts = jnp.sum(weights, axis=0, dtype=jnp.float32)
        owned_sums, owned_counts = (
            lax.psum_scatter(partial_sums, "dp", scatter_dimension=0, tiled=True),
            lax.psum_scatter(counts, "dp", scatter_dimension=0, tiled=True),
        )
        sum_parts.append(owned_sums)
        count_parts.append(owned_counts)
    own_sums = jnp.concatenate(sum_parts, axis=0)
    own_counts = jnp.concatenate(count_parts, axis=0)
    new_centroids = (own_sums + centroids) / (own_counts[:, None] + 1.0)
    own_points = points.shape[0]
    own_total = lax.dynamic_slice_in_dim(log_total, lax.axis_index("cent") * own_points, own_points)
    return (new_centroids, own_total)


def solution(mesh):
    placed = (P(("dp", "cent"), None), P(("dp", "cent"), None))
    return jax.shard_map(
        on_device,
        mesh=mesh,
        in_specs=placed,
        out_specs=(P(("dp", "cent"), None), P(("dp", "cent"))),
        check_vma=False,
    )
```

profile of v0, /device:TPU:1, one launch (start us, length us, event | category | flops | bytes accessed | tf_op | source)
XLA Modules:
  0.0 861.3 jit_solution(398983884775000078)
XLA Ops:
  7.2 0.7 all-gather.2.cloned.1.call-update
  7.9 0.0 reduce-scatter.5.cloned.1.call-start
  7.9 1.2 convert_element_type.35
  9.1 3.4 all_gather.7
  12.5 0.2 multiply_reduce_fusion.2
  12.7 0.2 multiply_reduce_fusion.3
  13.0 0.1 fusion.22
  13.0 91.7 %all-gather.2.cloned.1.call-done = bf16[8192,768]{1,0:T(8,128)(2,1)} async-done(((bf16[128,768]{1,0:T(8,128)(2,1)}), bf16[8192,768]{1,0:T(8,128)(2,1)}) %all-gather.2.cloned.1.call-update) | async-done | bytes 12582928 | tf_op jit(solution)/shard_map/all_gather | solution.py:33
  104.7 11.4 %fusion.23 = (f32[8192]{0:T(1024)S(1)}, f32[8192,256]{1,0:T(8,128)}) fusion(f32[256]{0:T(256)S(1)} %get-tuple-element.5, bf16[8192,768]{1,0:T(8,128)(2,1)} %all-gather.2.cloned.1.call-done, bf16[512,768]{1,0:T(8,128)(2,1)S(1)} %all_gather.7), kind=kOutput, calls=%fused_computation.39 | convolution fusion | flops 3229605888 | bytes 21398528 | tf_op jit(solution)/shard_map/dot_general | solution.py:12
  116.1 5.7 fusion.24
  121.9 291.5 %pmax.7 = bf16[8192]{0:T(1024)(128)(2,1)S(1)} all-reduce(bf16[8192]{0:T(1024)(128)(2,1)S(1)} %get-tuple-element.8), channel_id=1, replica_groups=mesh['dp'=2,'cent'=64] {'cent'}, use_global_device_ids=true, to_apply=%region_5.0 | all-reduce | flops 8192 | bytes 32768 | tf_op jit(solution)/shard_map/pmax | solution.py:48
  413.4 8.3 exponential_reduce_fusion
  421.7 286.7 %psum.7 = f32[8192]{0:T(1024)S(1)} all-reduce(f32[8192]{0:T(1024)S(1)} %fusion.18), channel_id=1, replica_groups=mesh['dp'=2,'cent'=64] {'cent'}, use_global_device_ids=true, to_apply=%region_8.0 | all-reduce | flops 8192 | bytes 65536 | tf_op jit(solution)/shard_map/psum | solution.py:49
  708.4 6.8 convert_reduce_fusion
  715.3 7.4 fusion.26
  722.7 0.2 reduce-scatter.3.cloned.1.call-start
  722.9 6.8 convert_reduce_fusion.1
  729.7 7.5 fusion.25
  737.3 0.6 dynamic-slice
  738.5 113.3 %all-reduce.2 = (f32[256]{0:T(256)S(1)}, f32[256]{0:T(256)S(1)}) all-reduce(f32[256]{0:T(256)S(1)} %get-tuple-element.17, f32[256]{0:T(256)S(1)} %get-tuple-element.19), channel_id=5, replica_groups=mesh['dp'=2,'cent'=64] {'dp'}, use_global_device_ids=true, to_apply=%region_15.0.clone | all-reduce | flops 512 | bytes 4096
  851.9 0.1 dynamic-slice.3
  851.9 0.1 dynamic-slice.1
  852.0 0.6 dynamic_slice.3
  852.7 2.1 fusion.14
  (15 shorter events, 0.2 us)
Async XLA Ops:
  7.2 97.6 %all-gather.2.cloned.1.call-start = ((), (), s32[]{:S(2)}) async-start(), calls=%async_computation.2 | async-start | bytes 12779520 | tf_op jit(solution)/shard_map/all_gather | solution.py:33
  7.9 844.7 %reduce-scatter.5.cloned.1.call-start = ((), (), s32[]{:S(2)}) async-start(), calls=%async_computation.4 | async-start | bytes 1179648 | tf_op jit(solution)/shard_map/reduce_scatter | solution.py:63
  104.7 11.4 %copy-start = (bf16[8192,768]{1,0:T(8,128)(2,1)S(1)}, bf16[8192,768]{1,0:T(8,128)(2,1)}, u32[]{:S(2)}) copy-start(bf16[8192,768]{1,0:T(8,128)(2,1)} %all-gather.2.cloned.1.call-done) | copy-start | bytes 37748740
  722.7 130.0 %reduce-scatter.3.cloned.1.call-start = ((), (), s32[]{:S(2)}) async-start(), calls=%async_computation.3 | async-start | bytes 1179648 | tf_op jit(solution)/shard_map/reduce_scatter | solution.py:63
  729.7 7.5 copy-start.2
  729.7 122.9 %copy-start.1 = (f32[256,768]{1,0:T(8,128)S(1)}, f32[256,768]{1,0:T(8,128)}, u32[]{:S(2)}) copy-start(f32[256,768]{1,0:T(8,128)} %param.3) | copy-start | bytes 2359300
Sparse Core Ops, SparseCore 0:
  10.7 93.9 all-gather.1
  722.8 114.9 reduce-scatter.4
  840.1 12.4 reduce-scatter.2
where the time goes:
time: 862 us; the launch traced here: 861 us
  blocking collectives  695 us (81%)
  waiting for transfers between devices  92.4 us (11%)
  matrix products  45.7 us (5%)
  between operations  14.5 us (2%)
  other arithmetic  12.1 us (1%)
    pmax x1, blocking collectives, on_device(): lax.pmax(local_max.astype(jnp.bfloat16), 'cent').astype(local_max.dtype)  292 us
    psum x1, blocking collectives, on_device(): global_sum = lax.psum(local_sum * jnp.exp(local_max - global_max), 'cent')  287 us
    unnamed x1, blocking collectives  113 us
    all_gather x1, waiting for transfers between devices, on_device(): members = lax.all_gather(points, 'cent', axis=0, tiled=True)  91.7 us
    dot_general x4, matrix products, score_block(): lax.dot_general(members, cent_block, (((1,), (1,)), ((), ())), preferred_...  30.8 us
  transfers between devices with their start and end apart: 3, of which 1 were waited for; matrix products, arithmetic and copies ran while one was open for 2% of the time, Pallas kernels for 0%

commit v1 on v0

--- a/solution.py
+++ b/solution.py
@@ -46,7 +46,9 @@
         )
     local_max, local_sum = running
     global_max = lax.pmax(local_max.astype(jnp.bfloat16), "cent").astype(local_max.dtype)
-    global_sum = lax.psum(local_sum * jnp.exp(local_max - global_max), "cent")
+    global_sum = jnp.sum(
+        lax.all_gather(local_sum * jnp.exp(local_max - global_max), "cent"), axis=0
+    )
     log_total = global_max + jnp.log(global_sum)
     arranged = gathered.reshape(dp_count, BLOCKS, part_rows, feature_width)
     sum_parts = []

time: 862 us -> 586 us (0.68)
  blocking collectives: 695 us -> 299 us
  waiting for transfers between devices: 92.4 us -> 209 us
    psum x1 -> x0, blocking collectives: 287 us -> none  [on_device(): global_sum = lax.psum(local_sum * jnp.exp(local_max - global_max), 'cent')]
    all_gather x0 -> x1, waiting for transfers between devices: none -> 112 us  [on_device(): lax.all_gather(local_sum * jnp.exp(local_max - global_max), 'cent')]
    unnamed x1, blocking collectives: 113 us -> 4.24 us
  transfers between devices with their start and end apart: 3 -> 4, of which waited for: 1 -> 3; matrix products, arithmetic and copies ran while one was open for 2% -> 3% of each run, Pallas kernels for 0% -> 0%
where the time goes in v1:
time: 586 us; the launch traced here: 585 us
  blocking collectives  299 us (51%)
  waiting for transfers between devices  209 us (36%)
  matrix products  46 us (8%)
  between operations  14.5 us (2%)
  other arithmetic  12.8 us (2%)
    pmax x1, blocking collectives, on_device(): lax.pmax(local_max.astype(jnp.bfloat16), 'cent').astype(local_max.dtype)  292 us
    all_gather x1, waiting for transfers between devices, on_device(): lax.all_gather(local_sum * jnp.exp(local_max - global_max), 'cent')  112 us
    all_gather x1, waiting for transfers between devices, on_device(): members = lax.all_gather(points, 'cent', axis=0, tiled=True)  92 us
    dot_general x4, matrix products, score_block(): lax.dot_general(members, cent_block, (((1,), (1,)), ((), ())), preferred_...  30.8 us
    dot_general x2, matrix products, on_device(): lax.dot_general(weights, members, (((0,), (0,)), ((), ())), preferred_ele...  15.2 us
  transfers between devices with their start and end apart: 4, of which 3 were waited for; matrix products, arithmetic and copies ran while one was open for 3% of the time, Pallas kernels for 0%

profile of v1, /device:TPU:1, one launch (start us, length us, event | category | flops | bytes accessed | tf_op | source)
XLA Modules:
  0.0 585.4 jit_solution(12936786160581797606)
XLA Ops:
  7.2 0.7 all-gather.4.cloned.1.call-update
  7.9 1.2 convert_element_type.35
  9.1 3.4 all_gather.13
  12.5 0.2 multiply_reduce_fusion.2
  12.7 92.0 %all-gather.4.cloned.1.call-done = bf16[8192,768]{1,0:T(8,128)(2,1)} async-done(((bf16[128,768]{1,0:T(8,128)(2,1)}), bf16[8192,768]{1,0:T(8,128)(2,1)}) %all-gather.4.cloned.1.call-update) | async-done | bytes 12582928 | tf_op jit(solution)/shard_map/all_gather | solution.py:33
  104.7 11.4 %fusion.23 = (f32[8192]{0:T(1024)S(1)}, f32[8192,256]{1,0:T(8,128)}) fusion(f32[256]{0:T(256)S(1)} %get-tuple-element.5, bf16[8192,768]{1,0:T(8,128)(2,1)} %all-gather.4.cloned.1.call-done, bf16[512,768]{1,0:T(8,128)(2,1)S(1)} %all_gather.13), kind=kOutput, calls=%fused_computation.39 | convolution fusion | flops 3229605888 | bytes 21398528 | tf_op jit(solution)/shard_map/dot_general | solution.py:12
  116.1 5.7 fusion.24
  121.9 291.5 %pmax.7 = bf16[8192]{0:T(1024)(128)(2,1)S(1)} all-reduce(bf16[8192]{0:T(1024)(128)(2,1)S(1)} %get-tuple-element.8), channel_id=1, replica_groups=mesh['dp'=2,'cent'=64] {'cent'}, use_global_device_ids=true, to_apply=%region_5.0 | all-reduce | flops 8192 | bytes 32768 | tf_op jit(solution)/shard_map/pmax | solution.py:48
  413.4 8.3 %exponential_reduce_fusion = (f32[8192]{0:T(1024)S(1)}, f32[8192]{0:T(1024)S(1)}) fusion(f32[8192,256]{1,0:T(8,128)} %get-tuple-element.14, f32[8192]{0:T(1024)S(1)} %get-tuple-element.9, f32[8192,256]{1,0:T(8,128)} %get-tuple-element.16, f32[8192]{0:T(1024)S(1)} %get-tuple-element.12), kind=kLoop, calls=%fused_computation.20 | loop fusion | flops 8372224 | bytes 16908288 | tf_op jit(solution)/shard_map/reduce_sum | solution.py:21
  421.7 0.6 fusion.18
  422.4 0.2 multiply_reduce_fusion.3
  422.6 0.8 fusion.22
  423.4 111.6 %all-gather.6.cloned.1.call-done = f32[524288]{0:T(1024)} async-done(((f32[8192]{0:T(1024)}), f32[524288]{0:T(1024)}) %all-gather.6.cloned.1.call-update) | async-done | bytes 2097168 | tf_op jit(solution)/shard_map/all_gather | solution.py:50
  535.0 1.7 reshape.45
  536.9 6.9 %convert_reduce_fusion = (f32[256]{0:T(256)S(1)}, bf16[8192,256]{1,0:T(8,128)(2,1)S(1)}) fusion(f32[8192]{0:T(1024)S(1)} %convert_add_fusion, f32[256]{0:T(256)S(1)} %bitcast.21, bf16[8192,768]{1,0:T(8,128)(2,1)} %all-gather.4.cloned.1.call-done, bf16[256,768]{1,0:T(8,128)(2,1)} %bitcast.19), kind=kOutput, calls=%fused_computation.18 | convolution fusion | flops 3235905280 | bytes 17205248 | tf_op jit(solution)/shard_map/dot_general | solution.py:12
  543.8 7.4 %fusion.26 = f32[256,768]{1,0:T(8,128)} fusion(bf16[8192,256]{1,0:T(8,128)(2,1)S(1)} %get-tuple-element.18, bf16[8192,768]{1,0:T(8,128)(2,1)} %all-gather.4.cloned.1.call-done), kind=kOutput, calls=%fused_computation.42 | convolution fusion | flops 3221225472 | bytes 17563648 | tf_op jit(solution)/shard_map/dot_general | solution.py:60
  551.2 0.2 reduce-scatter.3.cloned.1.call-start
  551.4 6.8 %convert_reduce_fusion.1 = (f32[256]{0:T(256)S(1)}, bf16[8192,256]{1,0:T(8,128)(2,1)S(1)}) fusion(f32[8192]{0:T(1024)S(1)} %convert_add_fusion, f32[256]{0:T(256)S(1)} %bitcast.20, bf16[8192,768]{1,0:T(8,128)(2,1)} %all-gather.4.cloned.1.call-done, bf16[256,768]{1,0:T(8,128)(2,1)S(1)} %bitcast.18), kind=kOutput, calls=%fused_computation.19 | convolution fusion | flops 3235905280 | bytes 17205248 | tf_op jit(solution)/shard_map/dot_general | solution.py:12
  558.2 7.9 %fusion.25 = f32[256,768]{1,0:T(8,128)} fusion(bf16[8192,256]{1,0:T(8,128)(2,1)S(1)} %get-tuple-element.20, bf16[8192,768]{1,0:T(8,128)(2,1)} %all-gather.4.cloned.1.call-done), kind=kOutput, calls=%fused_computation.41 | convolution fusion | flops 3221225472 | bytes 17563648 | tf_op jit(solution)/shard_map/dot_general | solution.py:60
  566.1 0.6 dynamic-slice
  567.4 4.2 all-reduce.2
  571.8 0.6 dynamic_slice.3
  572.4 4.3 reduce-scatter.3.cloned.1.call-done
  576.7 2.1 fusion.14
  (19 shorter events, 0.5 us)
Async XLA Ops:
  7.2 97.6 %all-gather.4.cloned.1.call-start = ((), (), s32[]{:S(2)}) async-start(), calls=%async_computation.2 | async-start | bytes 12779520 | tf_op jit(solution)/shard_map/all_gather | solution.py:33
  7.9 527.1 %all-gather.6.cloned.1.call-start = ((), (), s32[]{:S(2)}) async-start(), calls=%async_computation.5 | async-start | bytes 2129920 | tf_op jit(solution)/shard_map/all_gather | solution.py:50
  104.7 11.4 %copy-start = (bf16[8192,768]{1,0:T(8,128)(2,1)S(1)}, bf16[8192,768]{1,0:T(8,128)(2,1)}, u32[]{:S(2)}) copy-start(bf16[8192,768]{1,0:T(8,128)(2,1)} %all-gather.4.cloned.1.call-done) | copy-start | bytes 37748740
  422.3 150.1 %reduce-scatter.5.cloned.1.call-start = ((), (), s32[]{:S(2)}) async-start(), calls=%async_computation.4 | async-start | bytes 1179648 | tf_op jit(solution)/shard_map/reduce_scatter | solution.py:65
  551.2 25.6 %reduce-scatter.3.cloned.1.call-start = ((), (), s32[]{:S(2)}) async-start(), calls=%async_computation.3 | async-start | bytes 1179648 | tf_op jit(solution)/shard_map/reduce_scatter | solution.py:65
  558.2 7.9 %copy-start.2 = (u32[128]{0:T(128)S(1)}, u32[128]{0:T(128)}, u32[]{:S(2)}) copy-start(u32[128]{0:T(128)} %constant.25) | copy-start | bytes 1540
  558.2 18.5 %copy-start.1 = (f32[256,768]{1,0:T(8,128)S(1)}, f32[256,768]{1,0:T(8,128)}, u32[]{:S(2)}) copy-start(f32[256,768]{1,0:T(8,128)} %param.3) | copy-start | bytes 2359300
Sparse Core Ops, SparseCore 0:
  10.7 93.9 all-gather.3
  422.4 112.4 all-gather.5
  551.3 10.5 reduce-scatter.4
  566.2 10.4 reduce-scatter.2
